TPU v7x, 256 devices: a whole 4x4x8 slice. The times are simulated.
256 devices in a mesh: zone: 8 (over x, z_lo), brick: 32 (over z_hi, y, core).
Axes of the slice: x: 4, y: 4, z: 8 (z_hi: 4, z_lo: 2; z = z_hi * 2 + z_lo), core: 2. Of those that a mesh axis runs over, the one named last changes fastest.
Arguments:
- velocity: float32 [3, 2048, 64, 256], P(None, ('zone', 'brick')), may hold values from -3 to 3
- enthalpy: float32 [2048, 64, 256], P(('zone', 'brick')), may hold values from -6 to 6
- solvent: float32 [2048, 64, 256], P(('zone', 'brick')), may hold values from 0 to 1
- pressure: float32 [2048, 64, 256], P(('zone', 'brick')), may hold values from -6 to 6
- porosity: float32 [2048, 64, 256], P(('zone', 'brick')), may hold values from 0.1 to 1
- solid_mask: int32 [2048, 64, 256], P(('zone', 'brick')), may hold values 0 or 1
- nozzle_mask: int32 [2048, 256], P(('zone', 'brick')), may hold values 0 or 1
- zone_sizes: int32 [8], replicated, may hold values from 16 to 64, as said below
- zone_setpoint: float32 [8], replicated, may hold values from 0.5 to 2
- duct_source: int32 [256], P(('zone', 'brick')), may hold values from 0 to 7
- duct_span: int32 [256, 2], P(('zone', 'brick')), may hold values from 0 to 256, as said below
Outputs:
- velocity_new: float32 [3, 2048, 64, 256], P(None, ('zone', 'brick'))
- enthalpy_new: float32 [2048, 64, 256], P(('zone', 'brick'))
- solvent_new: float32 [2048, 64, 256], P(('zone', 'brick'))
- pressure_new: float32 [2048, 64, 256], P(('zone', 'brick'))
Inputs may be any that keep to these rules, and one draw needn't show every extreme that they name: `zone_sizes`: each zone's group holds a multiple of one thirty-second of all devices; the groups cover all devices, zone 0 first. duct_span[d,0] + duct_span[d,1] <= 256; duct_span[d,1] >= 64.
All inputs are finite; a program needn't handle non-finite values. No bound on the sum of `solid_mask` or of `nozzle_mask` on one device may be relied on, other than what follows from the above.
Results may differ from a plain program's by a relative error of at most 0.0003.
Values sent between devices are 32-bit elements; how exact they have to be, the bound alone decides.
No kernel may reach another device: no remote copies, remote signals or barrier semaphores. Data moves between devices by JAX's collectives and lax.ppermute only.
A program may use at most 128 MiB of HBM per device.

v0:
```python
import jax
import jax.numpy as jnp
from jax import lax
from jax.sharding import PartitionSpec as P

ITERS = 4
time_step = 0.2
viscosity = 0.1
diffusivity = 0.1
buoyancy = 0.5
evaporation = 0.5
latent_heat = 0.8
solvent_limit = 0.2


def extended(cells, sides, width):
    for axis, dim in sides:
        count = lax.axis_size(axis)
        ends = count - 1
        head = lax.slice_in_dim(cells, 0, width, axis=dim)
        tail = lax.slice_in_dim(cells, cells.shape[dim] - width, cells.shape[dim], axis=dim)
        cells = jnp.concatenate(
            [
                lax.ppermute(tail, axis, [(i, (i + 1) % count) for i in range(ends)]),
                cells,
                lax.ppermute(head, axis, [((i + 1) % count, i) for i in range(ends)]),
            ],
            axis=dim,
        )
    return cells


def shifted_down(values, axis):
    border = jnp.zeros_like(lax.slice_in_dim(values, 0, 1, axis=axis))
    inner = lax.slice_in_dim(values, 0, values.shape[axis] - 1, axis=axis)
    return jnp.concatenate([border, inner], axis=axis)


def shifted_up(values, axis):
    border = jnp.zeros_like(lax.slice_in_dim(values, 0, 1, axis=axis))
    inner = lax.slice_in_dim(values, 1, values.shape[axis], axis=axis)
    return jnp.concatenate([inner, border], axis=axis)


def momentum(vel_ext, pres_ext, heat_ext, poro_ext, components):
    open_here = poro_ext[1:-1]
    pressure_mid = pres_ext[1:-1]
    parts = []
    for component in components:
        values = vel_ext[component]
        centre = values[1:-1]
        laplacian = values[:-2] + values[2:] + shifted_down(centre, 1) + shifted_up(centre, 1)
        laplacian = laplacian + shifted_down(centre, 2) + shifted_up(centre, 2) - 6.0 * centre
        if component == 0:
            gradient = 0.5 * (pres_ext[2:] - pres_ext[:-2])
        else:
            gradient = 0.5 * (
                shifted_up(pressure_mid, component) - shifted_down(pressure_mid, component)
            )
        forcing = viscosity * laplacian - gradient
        if component == 1:
            forcing = forcing + buoyancy * heat_ext[1:-1]
        parts.append(open_here * (centre + time_step * forcing))
    return jnp.stack(parts)


def divergence_parts(first_ext, vel_star):
    result = 0.5 * (first_ext[2:] - first_ext[:-2])
    middle = vel_star[1]
    result = result + 0.5 * (shifted_up(middle, 1) - shifted_down(middle, 1))
    across = vel_star[2]
    return result + 0.5 * (shifted_up(across, 2) - shifted_down(across, 2))


def transport(scalar_ext, vel_star):
    centre = scalar_ext[1:-1]
    laplacian = scalar_ext[:-2] + scalar_ext[2:] + shifted_down(centre, 1) + shifted_up(centre, 1)
    laplacian = laplacian + shifted_down(centre, 2) + shifted_up(centre, 2) - 6.0 * centre
    advect = jnp.maximum(vel_star[0], 0.0) * (centre - scalar_ext[:-2]) + jnp.minimum(
        vel_star[0], 0.0
    ) * (scalar_ext[2:] - centre)
    for component in (1, 2):
        advect = advect + jnp.maximum(vel_star[component], 0.0) * (
            centre - shifted_down(centre, component)
        )
        advect = advect + jnp.minimum(vel_star[component], 0.0) * (
            shifted_up(centre, component) - centre
        )
    return centre + time_step * (diffusivity * laplacian - advect)


def sweep(pres_ext, open_ext, source):
    open_here = open_ext[1:-1]
    pressure_mid = pres_ext[1:-1]
    face_back = 0.5 * (open_here + open_ext[:-2])
    face_front = 0.5 * (open_here + open_ext[2:])
    numerator = face_back * pres_ext[:-2] + face_front * pres_ext[2:] - source
    denominator = face_back + face_front
    for component in (1, 2):
        face_low = 0.5 * (open_here + shifted_down(open_here, component))
        face_high = 0.5 * (open_here + shifted_up(open_here, component))
        numerator = (
            numerator
            + face_low * shifted_down(pressure_mid, component)
            + face_high * shifted_up(pressure_mid, component)
        )
        denominator = denominator + face_low + face_high
    inside = open_here > 0.0
    return jnp.where(inside, numerator / jnp.where(inside, denominator, 1.0), 0.0)


def on_device(
    velocity,
    enthalpy,
    solvent,
    pressure,
    porosity,
    solid_mask,
    nozzle_mask,
    zone_sizes,
    zone_setpoint,
    duct_source,
    duct_span,
):
    stacked = jnp.concatenate(
        [velocity, jnp.stack([enthalpy, solvent, pressure, porosity])], axis=0
    )
    padded = extended(stacked, ((("zone", "brick"), 1),), 1)
    heat_ext = padded[3]
    solv_ext = padded[4]
    poro_ext = padded[6]
    vel_star = momentum(padded[0:3], padded[5], padded[3], padded[6], (0, 1, 2))
    first_ext = extended(vel_star[0], ((("zone", "brick"), 0),), 1)
    source = divergence_parts(first_ext, vel_star) / time_step
    heat_new = transport(heat_ext, vel_star)
    solv_new = transport(solv_ext, vel_star)
    drying = time_step * evaporation * solid_mask.astype(jnp.float32) * solvent
    heat_new = heat_new - latent_heat * drying
    solv_new = solv_new - drying
    device = lax.axis_index(("zone", "brick"))
    starts = jnp.cumsum(zone_sizes) - zone_sizes
    zone_here = jnp.sum((device >= starts).astype(jnp.int32)) - 1
    choose = (jnp.arange(zone_sizes.shape[0], dtype=jnp.int32) == zone_here).astype(jnp.float32)
    totals = lax.psum(choose * jnp.sum(solvent[:, -1, :]), ("zone", "brick"))
    counts = zone_sizes.astype(jnp.float32) * (enthalpy.shape[0] * enthalpy.shape[2])
    means = totals / counts
    fresh_all = means / (means + solvent_limit)
    fresh = jnp.sum(choose * fresh_all)
    target = jnp.sum(choose * zone_setpoint)
    planes = jnp.stack([enthalpy[:, -1, :], solvent[:, -1, :]])[None]
    gathered = lax.all_gather(planes, "zone", axis=0, tiled=True)
    pick = (jnp.arange(gathered.shape[0], dtype=jnp.int32) == duct_source[0]).astype(jnp.float32)
    arrived = jnp.sum(pick[:, None, None, None] * gathered, axis=0)
    supply_heat = (1.0 - fresh) * arrived[0] + fresh * target
    supply_solv = (1.0 - fresh) * arrived[1]
    column = jnp.arange(enthalpy.shape[2], dtype=jnp.int32)
    inside_box = (column >= duct_span[0, 0]) & (column < duct_span[0, 0] + duct_span[0, 1])
    jets = (nozzle_mask > 0) & inside_box[None, :]
    heat_layer = jnp.where(jets, supply_heat, heat_new[:, 0, :])
    solv_layer = jnp.where(jets, supply_solv, solv_new[:, 0, :])
    enthalpy_new = jnp.concatenate([heat_layer[:, None, :], heat_new[:, 1:, :]], axis=1)
    solvent_new = jnp.concatenate([solv_layer[:, None, :], solv_new[:, 1:, :]], axis=1)
    iterate = pressure
    for iteration in range(ITERS):
        pres_ext = extended(iterate, ((("zone", "brick"), 0),), 1)
        iterate = sweep(pres_ext, poro_ext, source)
    pres_ext = extended(iterate, ((("zone", "brick"), 0),), 1)
    gradients = jnp.stack(
        [
            0.5 * (pres_ext[2:] - pres_ext[:-2]),
            0.5 * (shifted_up(iterate, 1) - shifted_down(iterate, 1)),
            0.5 * (shifted_up(iterate, 2) - shifted_down(iterate, 2)),
        ]
    )
    velocity_new = vel_star - time_step * porosity[None] * gradients
    return (velocity_new, enthalpy_new, solvent_new, iterate)


def solution(mesh):
    placed = (
        P(None, ("zone", "brick"), None, None),
        P(("zone", "brick"), None, None),
        P(("zone", "brick"), None, None),
        P(("zone", "brick"), None, None),
        P(("zone", "brick"), None, None),
        P(("zone", "brick"), None, None),
        P(("zone", "brick"), None),
        P(),
        P(),
        P(("zone", "brick")),
        P(("zone", "brick"), None),
    )
    return jax.shard_map(
        on_device,
        mesh=mesh,
        in_specs=placed,
        out_specs=(
            P(None, ("zone", "brick"), None, None),
            P(("zone", "brick"), None, None),
            P(("zone", "brick"), None, None),
            P(("zone", "brick"), None, None),
        ),
        check_vma=False,
    )
```

profile of v0, /device:TPU:32, one launch (start us, length us, event | category | flops | bytes accessed | tf_op | source)
XLA Modules:
  0.0 256.3 jit_solution(2717288666460999411)
XLA Ops:
  0.7 2.4 fusion.106
  6.7 1.9 collective-permute-start
  8.6 9.6 %collective-permute-start.1 = (f32[7,1,64,256]{3,1,2,0:T(1,128)}, f32[7,1,64,256]{3,1,2,0:T(1,128)}, u32[]{:S(2)}, u32[]{:S(2)}) collective-permute-start(f32[7,1,64,256]{3,1,2,0:T(1,128)} %get-tuple-element.31), channel_id=1, source_target_pairs={{1,0},{2,1},{3,2},{4,3},{5,4},{6,5},{7,6},{8,7},{9,8},{10,9},{11,1... | collective-permute-start | bytes 1376264 | tf_op jit(solution)/shard_map/ppermute | solution.py:26
  18.3 1.9 collective-permute-start.2
  20.3 8.8 %collective-permute-start.3 = (f32[1,64,256]{2,0,1:T(1,128)S(1)}, f32[1,64,256]{2,0,1:T(1,128)S(1)}, u32[]{:S(2)}, u32[]{:S(2)}) collective-permute-start(f32[1,64,256]{2,0,1:T(1,128)S(1)} %copy.188), channel_id=1, source_target_pairs={{1,0},{2,1},{3,2},{4,3},{5,4},{6,5},{7,6},{8,7},{9,8},{10,9},{11,1... | collective-permute-start | bytes 196616 | tf_op jit(solution)/shard_map/ppermute | solution.py:26
  45.2 74.0 %psum.7 = f32[8]{0:T(128)S(1)} all-reduce(f32[8]{0:T(128)S(1)} %fusion.98), channel_id=1, replica_groups=mesh['zone'=8,'brick'=32] {'zone','brick'}, use_global_device_ids=true, to_apply=%region_3.4 | all-reduce | flops 8 | bytes 64 | tf_op jit(solution)/shard_map/psum | solution.py:144
  119.9 26.4 %all-gather = f32[16,8,256]{2,1,0:T(8,128)S(1)} all-gather(f32[2,8,256]{2,1,0:T(8,128)S(1)} %pad_maximum_fusion.16), channel_id=2, replica_groups=mesh['zone'=8,'brick'=32] {'zone'}, dimensions={0}, use_global_device_ids=true | all-gather | bytes 147456 | tf_op jit(solution)/shard_map/all_gather | solution.py:151
  153.0 2.2 copy.269
  155.2 2.2 copy.270
  164.2 6.4 %add_subtract_fusion = (f32[8,64,256]{2,0,1:T(8,128)S(1)}, f32[8,64,256]{2,0,1:T(8,128)S(1)}, f32[8,64,256]{2,0,1:T(8,128)S(1)}, f32[8,64,256]{2,0,1:T(8,128)S(1)}) fusion(f32[8,64,255]{2,0,1:T(8,128)S(1)} %get-tuple-element.108, f32[8,64,255]{2,0,1:T(8,128)S(1)} %get-tuple-element.109, f32[8,63,256]{2,0,1:T(8,128)} %get-tuple-element.106, ...), kind=kLoop, calls=%fused_computation.125 | loop fusion | flops 12058624 | bytes 20738048 | tf_op jit(solution)/shard_map/sub | solution.py:139
  173.6 2.6 %multiply_subtract_fusion = f32[8,64,256]{2,0,1:T(8,128)S(1)} fusion(f32[8,64,255]{2,0,1:T(8,128)S(1)} %copy-done.18, f32[8,64,255]{2,0,1:T(8,128)S(1)} %copy-done.17, f32[8,63,256]{2,0,1:T(8,128)S(1)} %copy-done.22, f32[8,63,256]{2,0,1:T(8,128)S(1)} %copy-done.21, f32[7,8,64,256]{3,1,2,0:T(8,128)S(1)} %copy-done.1, ...), kind=kLoop, calls=%fused_computation.126 | loop fusion | flops 5373952 | bytes 10334208 | tf_op jit(solution)/shard_map/sub | solution.py:138
  176.3 2.2 collective-permute-start.4
  178.5 2.4 collective-permute-start.5
  181.9 8.0 %collective-permute-done.5 = f32[1,64,256]{2,0,1:T(1,128)S(1)} collective-permute-done((f32[1,64,256]{2,0,1:T(1,128)S(1)}, f32[1,64,256]{2,0,1:T(1,128)S(1)}, u32[]{:S(2)}, u32[]{:S(2)}) %collective-permute-start.5) | collective-permute-done | bytes 65568 | tf_op jit(solution)/shard_map/ppermute | solution.py:24
  189.9 2.5 fusion.47
  192.8 1.9 collective-permute-start.6
  194.7 8.8 %collective-permute-start.7 = (f32[1,64,256]{2,0,1:T(1,128)S(1)}, f32[1,64,256]{2,0,1:T(1,128)S(1)}, u32[]{:S(2)}, u32[]{:S(2)}) collective-permute-start(f32[1,64,256]{2,0,1:T(1,128)S(1)} %get-tuple-element.67), channel_id=1, source_target_pairs={{1,0},{2,1},{3,2},{4,3},{5,4},{6,5},{7,6},{8,7},{9,8},{10,9},{11,1... | collective-permute-start | bytes 196616 | tf_op jit(solution)/shard_map/ppermute | solution.py:26
  206.3 1.9 collective-permute-start.8
  208.2 8.8 %collective-permute-start.9 = (f32[1,64,256]{2,0,1:T(1,128)S(1)}, f32[1,64,256]{2,0,1:T(1,128)S(1)}, u32[]{:S(2)}, u32[]{:S(2)}) collective-permute-start(f32[1,64,256]{2,0,1:T(1,128)S(1)} %get-tuple-element.61), channel_id=1, source_target_pairs={{1,0},{2,1},{3,2},{4,3},{5,4},{6,5},{7,6},{8,7},{9,8},{10,9},{11,1... | collective-permute-start | bytes 196616 | tf_op jit(solution)/shard_map/ppermute | solution.py:26
  219.9 1.9 collective-permute-start.10
  221.8 9.0 %collective-permute-start.11 = (f32[1,64,256]{2,0,1:T(1,128)S(1)}, f32[1,64,256]{2,0,1:T(1,128)S(1)}, u32[]{:S(2)}, u32[]{:S(2)}) collective-permute-start(f32[1,64,256]{2,0,1:T(1,128)S(1)} %get-tuple-element.55), channel_id=1, source_target_pairs={{1,0},{2,1},{3,2},{4,3},{5,4},{6,5},{7,6},{8,7},{9,8},{10,9},{11,1... | collective-permute-start | bytes 196616 | tf_op jit(solution)/shard_map/ppermute | solution.py:26
  234.6 8.8 %collective-permute-start.12 = (f32[1,64,256]{2,0,1:T(1,128)S(1)}, f32[1,64,256]{2,0,1:T(1,128)S(1)}, u32[]{:S(2)}, u32[]{:S(2)}) collective-permute-start(f32[1,64,256]{2,0,1:T(1,128)S(1)} %get-tuple-element.44), channel_id=1, source_target_pairs={{1,0},{2,1},{3,2},{4,3},{5,4},{6,5},{7,6},{8,7},{9,8},{10,9},{11,1... | collective-permute-start | bytes 196616 | tf_op jit(solution)/shard_map/ppermute | solution.py:26
  243.4 1.9 collective-permute-start.13
  245.6 8.5 %collective-permute-done.13 = f32[1,64,256]{2,0,1:T(1,128)S(1)} collective-permute-done((f32[1,64,256]{2,0,1:T(1,128)S(1)}, f32[1,64,256]{2,0,1:T(1,128)S(1)}, u32[]{:S(2)}, u32[]{:S(2)}) %collective-permute-start.13) | collective-permute-done | bytes 65568 | tf_op jit(solution)/shard_map/ppermute | solution.py:24
  (136 shorter events, 45.3 us)
Async XLA Ops:
  4.7 24.5 %copy-start = (f32[7,8,64,256]{3,1,2,0:T(8,128)}, f32[7,8,64,256]{3,1,2,0:T(8,128)S(1)}, u32[]{:S(2)}) copy-start(f32[7,8,64,256]{3,1,2,0:T(8,128)S(1)} %bitcast_dynamic-update-slice_fusion) | copy-start | bytes 11010052
  6.7 156.8 %collective-permute-start = (f32[7,1,64,256]{3,1,2,0:T(1,128)}, f32[7,1,64,256]{3,1,2,0:T(1,128)}, u32[]{:S(2)}, u32[]{:S(2)}) collective-permute-start(f32[7,1,64,256]{3,1,2,0:T(1,128)} %get-tuple-element.32), channel_id=1, source_target_pairs={{0,1},{1,2},{2,3},{3,4},{4,5},{5,6},{6,7},{7,8},{8,9},{9,10},{10,1... | collective-permute-start | bytes 1376264 | tf_op jit(solution)/shard_map/ppermute | solution.py:24
  8.6 154.8 %collective-permute-start.1 = (f32[7,1,64,256]{3,1,2,0:T(1,128)}, f32[7,1,64,256]{3,1,2,0:T(1,128)}, u32[]{:S(2)}, u32[]{:S(2)}) collective-permute-start(f32[7,1,64,256]{3,1,2,0:T(1,128)} %get-tuple-element.31), channel_id=1, source_target_pairs={{1,0},{2,1},{3,2},{4,3},{5,4},{6,5},{7,6},{8,7},{9,8},{10,9},{11,1... | collective-permute-start | bytes 1376264 | tf_op jit(solution)/shard_map/ppermute | solution.py:26
  18.3 163.6 %collective-permute-start.2 = (f32[1,64,256]{2,0,1:T(1,128)S(1)}, f32[1,64,256]{2,0,1:T(1,128)S(1)}, u32[]{:S(2)}, u32[]{:S(2)}) collective-permute-start(f32[1,64,256]{2,0,1:T(1,128)S(1)} %copy.185), channel_id=1, source_target_pairs={{0,1},{1,2},{2,3},{3,4},{4,5},{5,6},{6,7},{7,8},{8,9},{9,10},{10,1... | collective-permute-start | bytes 196616 | tf_op jit(solution)/shard_map/ppermute | solution.py:24
  20.3 161.6 %collective-permute-start.3 = (f32[1,64,256]{2,0,1:T(1,128)S(1)}, f32[1,64,256]{2,0,1:T(1,128)S(1)}, u32[]{:S(2)}, u32[]{:S(2)}) collective-permute-start(f32[1,64,256]{2,0,1:T(1,128)S(1)} %copy.188), channel_id=1, source_target_pairs={{1,0},{2,1},{3,2},{4,3},{5,4},{6,5},{7,6},{8,7},{9,8},{10,9},{11,1... | collective-permute-start | bytes 196616 | tf_op jit(solution)/shard_map/ppermute | solution.py:26
  29.2 11.4 %copy-start.3 = (f32[8,64,256]{2,0,1:T(8,128)}, f32[8,64,256]{2,0,1:T(8,128)S(1)}, u32[]{:S(2)}) copy-start(f32[8,64,256]{2,0,1:T(8,128)S(1)} %get-tuple-element.35) | copy-start | bytes 1572868
  173.6 16.3 %copy-start.23 = (f32[8,63,256]{2,0,1:T(8,128)S(1)}, f32[8,63,256]{2,0,1:T(8,128)}, u32[]{:S(2)}) copy-start(f32[8,63,256]{2,0,1:T(8,128)} %copy.271) | copy-start | bytes 1548292
  173.6 16.3 %copy-start.24 = (f32[8,63,256]{2,0,1:T(8,128)S(1)}, f32[8,63,256]{2,0,1:T(8,128)}, u32[]{:S(2)}) copy-start(f32[8,63,256]{2,0,1:T(8,128)} %copy.272) | copy-start | bytes 1548292
  176.2 13.7 %copy-start.8 = (f32[8,64,255]{2,0,1:T(8,128)S(1)}, f32[8,64,255]{2,0,1:T(8,128)}, u32[]{:S(2)}) copy-start(f32[8,64,255]{2,0,1:T(8,128)} %get-tuple-element.84) | copy-start | bytes 1566724
  176.2 13.7 %copy-start.9 = (f32[8,64,255]{2,0,1:T(8,128)S(1)}, f32[8,64,255]{2,0,1:T(8,128)}, u32[]{:S(2)}) copy-start(f32[8,64,255]{2,0,1:T(8,128)} %get-tuple-element.85) | copy-start | bytes 1566724
  176.2 13.7 %copy-start.10 = (f32[8,63,256]{2,0,1:T(8,128)S(1)}, f32[8,63,256]{2,0,1:T(8,128)}, u32[]{:S(2)}) copy-start(f32[8,63,256]{2,0,1:T(8,128)} %get-tuple-element.90) | copy-start | bytes 1548292
  176.2 13.7 %copy-start.11 = (f32[8,63,256]{2,0,1:T(8,128)S(1)}, f32[8,63,256]{2,0,1:T(8,128)}, u32[]{:S(2)}) copy-start(f32[8,63,256]{2,0,1:T(8,128)} %get-tuple-element.91) | copy-start | bytes 1548292
  176.2 13.7 %copy-start.15 = (f32[8,64,255]{2,0,1:T(8,128)S(1)}, f32[8,64,255]{2,0,1:T(8,128)}, u32[]{:S(2)}) copy-start(f32[8,64,255]{2,0,1:T(8,128)} %copy.269) | copy-start | bytes 1566724
  176.2 13.7 %copy-start.16 = (f32[8,64,255]{2,0,1:T(8,128)S(1)}, f32[8,64,255]{2,0,1:T(8,128)}, u32[]{:S(2)}) copy-start(f32[8,64,255]{2,0,1:T(8,128)} %copy.270) | copy-start | bytes 1566724
  176.3 5.6 %collective-permute-start.4 = (f32[1,64,256]{2,0,1:T(1,128)S(1)}, f32[1,64,256]{2,0,1:T(1,128)S(1)}, u32[]{:S(2)}, u32[]{:S(2)}) collective-permute-start(f32[1,64,256]{2,0,1:T(1,128)S(1)} %get-tuple-element.68), channel_id=1, source_target_pairs={{1,0},{2,1},{3,2},{4,3},{5,4},{6,5},{7,6},{8,7},{9,8},{10,9},{11,1... | collective-permute-start | bytes 196616 | tf_op jit(solution)/shard_map/ppermute | solution.py:26
  178.5 11.4 %collective-permute-start.5 = (f32[1,64,256]{2,0,1:T(1,128)S(1)}, f32[1,64,256]{2,0,1:T(1,128)S(1)}, u32[]{:S(2)}, u32[]{:S(2)}) collective-permute-start(f32[1,64,256]{2,0,1:T(1,128)S(1)} %get-tuple-element.69), channel_id=1, source_target_pairs={{0,1},{1,2},{2,3},{3,4},{4,5},{5,6},{6,7},{7,8},{8,9},{9,10},{10,1... | collective-permute-start | bytes 196616 | tf_op jit(solution)/shard_map/ppermute | solution.py:24
  192.8 10.8 %collective-permute-start.6 = (f32[1,64,256]{2,0,1:T(1,128)S(1)}, f32[1,64,256]{2,0,1:T(1,128)S(1)}, u32[]{:S(2)}, u32[]{:S(2)}) collective-permute-start(f32[1,64,256]{2,0,1:T(1,128)S(1)} %get-tuple-element.66), channel_id=1, source_target_pairs={{0,1},{1,2},{2,3},{3,4},{4,5},{5,6},{6,7},{7,8},{8,9},{9,10},{10,1... | collective-permute-start | bytes 196616 | tf_op jit(solution)/shard_map/ppermute | solution.py:24
  194.7 10.7 %collective-permute-start.7 = (f32[1,64,256]{2,0,1:T(1,128)S(1)}, f32[1,64,256]{2,0,1:T(1,128)S(1)}, u32[]{:S(2)}, u32[]{:S(2)}) collective-permute-start(f32[1,64,256]{2,0,1:T(1,128)S(1)} %get-tuple-element.67), channel_id=1, source_target_pairs={{1,0},{2,1},{3,2},{4,3},{5,4},{6,5},{7,6},{8,7},{9,8},{10,9},{11,1... | collective-permute-start | bytes 196616 | tf_op jit(solution)/shard_map/ppermute | solution.py:26
  206.3 10.8 %collective-permute-start.8 = (f32[1,64,256]{2,0,1:T(1,128)S(1)}, f32[1,64,256]{2,0,1:T(1,128)S(1)}, u32[]{:S(2)}, u32[]{:S(2)}) collective-permute-start(f32[1,64,256]{2,0,1:T(1,128)S(1)} %get-tuple-element.60), channel_id=1, source_target_pairs={{0,1},{1,2},{2,3},{3,4},{4,5},{5,6},{6,7},{7,8},{8,9},{9,10},{10,1... | collective-permute-start | bytes 196616 | tf_op jit(solution)/shard_map/ppermute | solution.py:24
  208.2 10.7 %collective-permute-start.9 = (f32[1,64,256]{2,0,1:T(1,128)S(1)}, f32[1,64,256]{2,0,1:T(1,128)S(1)}, u32[]{:S(2)}, u32[]{:S(2)}) collective-permute-start(f32[1,64,256]{2,0,1:T(1,128)S(1)} %get-tuple-element.61), channel_id=1, source_target_pairs={{1,0},{2,1},{3,2},{4,3},{5,4},{6,5},{7,6},{8,7},{9,8},{10,9},{11,1... | collective-permute-start | bytes 196616 | tf_op jit(solution)/shard_map/ppermute | solution.py:26
  219.9 11.0 %collective-permute-start.10 = (f32[1,64,256]{2,0,1:T(1,128)S(1)}, f32[1,64,256]{2,0,1:T(1,128)S(1)}, u32[]{:S(2)}, u32[]{:S(2)}) collective-permute-start(f32[1,64,256]{2,0,1:T(1,128)S(1)} %get-tuple-element.54), channel_id=1, source_target_pairs={{0,1},{1,2},{2,3},{3,4},{4,5},{5,6},{6,7},{7,8},{8,9},{9,10},{10,1... | collective-permute-start | bytes 196616 | tf_op jit(solution)/shard_map/ppermute | solution.py:24
  221.8 10.7 %collective-permute-start.11 = (f32[1,64,256]{2,0,1:T(1,128)S(1)}, f32[1,64,256]{2,0,1:T(1,128)S(1)}, u32[]{:S(2)}, u32[]{:S(2)}) collective-permute-start(f32[1,64,256]{2,0,1:T(1,128)S(1)} %get-tuple-element.55), channel_id=1, source_target_pairs={{1,0},{2,1},{3,2},{4,3},{5,4},{6,5},{7,6},{8,7},{9,8},{10,9},{11,1... | collective-permute-start | bytes 196616 | tf_op jit(solution)/shard_map/ppermute | solution.py:26
  234.6 11.1 %collective-permute-start.12 = (f32[1,64,256]{2,0,1:T(1,128)S(1)}, f32[1,64,256]{2,0,1:T(1,128)S(1)}, u32[]{:S(2)}, u32[]{:S(2)}) collective-permute-start(f32[1,64,256]{2,0,1:T(1,128)S(1)} %get-tuple-element.44), channel_id=1, source_target_pairs={{1,0},{2,1},{3,2},{4,3},{5,4},{6,5},{7,6},{8,7},{9,8},{10,9},{11,1... | collective-permute-start | bytes 196616 | tf_op jit(solution)/shard_map/ppermute | solution.py:26
  243.4 10.7 %collective-permute-start.13 = (f32[1,64,256]{2,0,1:T(1,128)S(1)}, f32[1,64,256]{2,0,1:T(1,128)S(1)}, u32[]{:S(2)}, u32[]{:S(2)}) collective-permute-start(f32[1,64,256]{2,0,1:T(1,128)S(1)} %get-tuple-element.45), channel_id=1, source_target_pairs={{0,1},{1,2},{2,3},{3,4},{4,5},{5,6},{6,7},{7,8},{8,9},{9,10},{10,1... | collective-permute-start | bytes 196616 | tf_op jit(solution)/shard_map/ppermute | solution.py:24
  (17 other events, 47.6 us)
where the time goes:
time: 257 us; the launch traced here: 256 us
  blocking collectives  100 us (39%)
  starting transfers between devices  69.9 us (27%)
  local copies, waits for them, and re-layouts  36.6 us (14%)
  other arithmetic  21.9 us (9%)
  waiting for transfers between devices  21.6 us (8%)
  between operations  5.9 us (2%)
    psum x1, blocking collectives, on_device(): totals = lax.psum(choose * jnp.sum(solvent[:, -1, :]), ('zone', 'brick'))  74 us
    ppermute x7, starting transfers between devices, extended(): lax.ppermute(head, axis, [((i + 1) % count, i) for i in range(ends)])  56 us
    all_gather x1, blocking collectives, on_device(): gathered = lax.all_gather(planes, 'zone', axis=0, tiled=True)  26.4 us
    unnamed x70, local copies, waits for them, and re-layouts  18.1 us
    ppermute x7, waiting for transfers between devices, extended(): lax.ppermute(tail, axis, [(i, (i + 1) % count) for i in range(ends)])  16.4 us
    ppermute x7, starting transfers between devices, extended(): lax.ppermute(tail, axis, [(i, (i + 1) % count) for i in range(ends)])  13.9 us
    slice x12, local copies, waits for them, and re-layouts, shifted_down(): inner = lax.slice_in_dim(values, 0, values.shape[axis] - 1, axis=axis)  9.19 us
    sub x1, other arithmetic, on_device(): solv_new = solv_new - drying  6.42 us
  transfers between devices with their start and end apart: 14, of which 5 were waited for; matrix products, arithmetic and copies ran while one was open for 16% of the time, Pallas kernels for 0%

commit v1 on v0

--- a/solution.py
+++ b/solution.py
@@ -148,7 +148,9 @@
     fresh = jnp.sum(choose * fresh_all)
     target = jnp.sum(choose * zone_setpoint)
     planes = jnp.stack([enthalpy[:, -1, :], solvent[:, -1, :]])[None]
-    gathered = lax.all_gather(planes, "zone", axis=0, tiled=True)
+    gathered = jnp.concatenate(
+        lax.all_to_all(jnp.stack([planes] * lax.axis_size("zone")), "zone", 0, 0), axis=0
+    )
     pick = (jnp.arange(gathered.shape[0], dtype=jnp.int32) == duct_source[0]).astype(jnp.float32)
     arrived = jnp.sum(pick[:, None, None, None] * gathered, axis=0)
     supply_heat = (1.0 - fresh) * arrived[0] + fresh * target

time: 257 us -> 249 us (0.969)
  blocking collectives: 100 us -> 74 us
  local copies, waits for them, and re-layouts: 36.6 us -> 46.6 us
  starting transfers between devices: 69.9 us -> 76.1 us
  other arithmetic: 21.9 us -> 25.3 us
    all_gather x1 -> x0, blocking collectives: 26.4 us -> none  [on_device(): gathered = lax.all_gather(planes, 'zone', axis=0, tiled=True)]
    unnamed x70 -> x100, local copies, waits for them, and re-layouts: 18.1 us -> 27.8 us
    add x0 -> x2, other arithmetic: none -> 7.21 us  [the longest x1 4.38 us: transport(): advect + jnp.maximum(vel_star[component], 0.0) * (centre - shifted_down(c...]
    all_to_all x0 -> x1, starting transfers between devices: none -> 5.76 us  [on_device(): lax.all_to_all(jnp.stack([planes] * lax.axis_size('zone')), 'zone', 0, 0)]
    sub x1, other arithmetic: 6.42 us -> 0.72 us  [on_device(): solv_new = solv_new - drying]
    slice x12 -> x13, local copies, waits for them, and re-layouts: 9.19 us -> 7.15 us  [shifted_down(): inner = lax.slice_in_dim(values, 0, values.shape[axis] - 1, axis=axis)]
  transfers between devices with their start and end apart: 14 -> 15, of which waited for: 5 -> 5; matrix products, arithmetic and copies ran while one was open for 16% -> 21% of each run, Pallas kernels for 0% -> 0%
where the time goes in v1:
time: 249 us; the launch traced here: 248 us
  starting transfers between devices  76.1 us (31%)
  blocking collectives  74 us (30%)
  local copies, waits for them, and re-layouts  46.6 us (19%)
  other arithmetic  25.3 us (10%)
  waiting for transfers between devices  20.3 us (8%)
  between operations  5.96 us (2%)
    psum x1, blocking collectives, on_device(): totals = lax.psum(choose * jnp.sum(solvent[:, -1, :]), ('zone', 'brick'))  74 us
    ppermute x7, starting transfers between devices, extended(): lax.ppermute(head, axis, [((i + 1) % count, i) for i in range(ends)])  56.7 us
    unnamed x100, local copies, waits for them, and re-layouts  27.8 us
    ppermute x7, waiting for transfers between devices, extended(): lax.ppermute(tail, axis, [(i, (i + 1) % count) for i in range(ends)])  14.9 us
    ppermute x7, starting transfers between devices, extended(): lax.ppermute(tail, axis, [(i, (i + 1) % count) for i in range(ends)])  13.7 us
    slice x13, local copies, waits for them, and re-layouts, shifted_down(): inner = lax.slice_in_dim(values, 0, values.shape[axis] - 1, axis=axis)  7.15 us
    all_to_all x1, starting transfers between devices, on_device(): lax.all_to_all(jnp.stack([planes] * lax.axis_size('zone')), 'zone', 0, 0)  5.76 us
    ppermute x7, waiting for transfers between devices, extended(): lax.ppermute(head, axis, [((i + 1) % count, i) for i in range(ends)])  5.4 us
  transfers between devices with their start and end apart: 15, of which 5 were waited for; matrix products, arithmetic and copies ran while one was open for 21% of the time, Pallas kernels for 0%

profile of v1, /device:TPU:32, one launch (start us, length us, event | category | flops | bytes accessed | tf_op | source)
XLA Modules:
  0.0 248.3 jit_solution(11255940481475490986)
XLA Ops:
  0.7 2.4 fusion.114
  10.5 9.6 %collective-permute-start.1 = (f32[7,1,64,256]{3,1,2,0:T(1,128)}, f32[7,1,64,256]{3,1,2,0:T(1,128)}, u32[]{:S(2)}, u32[]{:S(2)}) collective-permute-start(f32[7,1,64,256]{3,1,2,0:T(1,128)} %get-tuple-element.33), channel_id=1, source_target_pairs={{1,0},{2,1},{3,2},{4,3},{5,4},{6,5},{7,6},{8,7},{9,8},{10,9},{11,1... | collective-permute-start | bytes 1376264 | tf_op jit(solution)/shard_map/ppermute | solution.py:26
  21.5 5.8 %all-to-all-start = ((f32[8,1,2,8,256]{4,3,2,1,0:T(8,128)}), f32[8,1,2,8,256]{4,3,2,1,0:T(8,128)S(1)}, u32[]{:S(2)}, u32[]{:S(2)}) async-start(f32[8,1,2,8,256]{4,3,2,1,0:T(8,128)} %stack.55), calls=%async_computation | async-start | bytes 262144 | tf_op jit(solution)/shard_map/all_to_all | solution.py:152
  28.2 1.9 collective-permute-start.2
  30.2 8.8 %collective-permute-start.3 = (f32[1,64,256]{2,0,1:T(1,128)S(1)}, f32[1,64,256]{2,0,1:T(1,128)S(1)}, u32[]{:S(2)}, u32[]{:S(2)}) collective-permute-start(f32[1,64,256]{2,0,1:T(1,128)S(1)} %copy.125), channel_id=1, source_target_pairs={{1,0},{2,1},{3,2},{4,3},{5,4},{6,5},{7,6},{8,7},{9,8},{10,9},{11,1... | collective-permute-start | bytes 196616 | tf_op jit(solution)/shard_map/ppermute | solution.py:26
  60.0 2.1 copy.306
  62.1 74.0 %psum.7 = f32[8]{0:T(128)S(1)} all-reduce(f32[8]{0:T(128)} %fusion.104), channel_id=1, replica_groups=mesh['zone'=8,'brick'=32] {'zone','brick'}, use_global_device_ids=true, to_apply=%region_3.4 | all-reduce | flops 8 | bytes 64 | tf_op jit(solution)/shard_map/psum | solution.py:144
  140.6 2.2 copy.299
  142.8 2.2 copy.300
  151.3 2.8 %fusion.61 = f32[8,64,256]{2,0,1:T(8,128)S(1)} fusion(f32[7,1,64,256]{3,1,2,0:T(1,128)} %collective-permute-done.1, f32[7,8,64,256]{3,1,2,0:T(8,128)} %copy-done, f32[7,1,64,256]{3,1,2,0:T(1,128)} %collective-permute-done, f32[8,64,255]{2,0,1:T(8,128)} %get-tuple-element.102, f32[8,64,255]{2,0,1:T(8,128)} %get-tuple-element.101, ...), kind=kLoop, calls=%fused_computation.82 | loop fusion | flops 1966080 | bytes 8757248 | tf_op jit(solution)/shard_map/add | solution.py:63
  156.7 4.4 %multiply_add_fusion = (f32[8,64,256]{2,0,1:T(8,128)S(1)}, f32[8,64,256]{2,0,1:T(8,128)S(1)}, f32[8,64,256]{2,0,1:T(8,128)S(1)}, f32[8,64,256]{2,0,1:T(8,128)S(1)}, f32[8,64,256]{2,0,1:T(8,128)S(1)}) fusion(f32[8,63,256]{2,0,1:T(8,128)S(1)} %copy-done.11, f32[8,63,256]{2,0,1:T(8,128)S(1)} %copy-done.12, f32[8,64,255]{2,0,1:T(8,128)S(1)} %copy.310, ...), kind=kLoop, calls=%fused_computation.137 | loop fusion | flops 7471104 | bytes 17094656 | tf_op jit(solution)/shard_map/add | solution.py:83
  162.8 3.2 %fusion.95 = (f32[8,64,256]{2,0,1:T(8,128)S(1)}, f32[8,64,256]{2,0,1:T(8,128)S(1)}) fusion(f32[8,64,256]{2,1,0:T(8,128)S(1)} %get-tuple-element.21, f32[8,64,255]{2,0,1:T(8,128)S(1)} %copy-done.18, f32[8,64,255]{2,0,1:T(8,128)S(1)} %copy-done.19, f32[8,63,256]{2,0,1:T(8,128)S(1)} %copy-done.30, f32[8,63,256]{2,0,1:T(8,128)S(1)} %copy-done.31, ...), kind=kLoop, calls=%fused_computation.134 | loop fusion | flops 5242880 | bytes 11382784 | tf_op jit(solution)/shard_map/sub | solution.py:138
  168.6 3.1 %collective-permute-start.4 = (f32[1,64,256]{2,0,1:T(1,128)S(1)}, f32[1,64,256]{2,0,1:T(1,128)S(1)}, u32[]{:S(2)}, u32[]{:S(2)}) collective-permute-start(f32[1,64,256]{2,0,1:T(1,128)S(1)} %get-tuple-element.73), channel_id=1, source_target_pairs={{1,0},{2,1},{3,2},{4,3},{5,4},{6,5},{7,6},{8,7},{9,8},{10,9},{11,1... | collective-permute-start | bytes 196616 | tf_op jit(solution)/shard_map/ppermute | solution.py:26
  171.7 2.1 collective-permute-start.5
  175.7 6.7 %collective-permute-done.5 = f32[1,64,256]{2,0,1:T(1,128)S(1)} collective-permute-done((f32[1,64,256]{2,0,1:T(1,128)S(1)}, f32[1,64,256]{2,0,1:T(1,128)S(1)}, u32[]{:S(2)}, u32[]{:S(2)}) %collective-permute-start.5) | collective-permute-done | bytes 65568 | tf_op jit(solution)/shard_map/ppermute | solution.py:24
  182.5 2.5 %fusion.46 = (f32[8,64,256]{2,0,1:T(8,128)S(1)}, f32[8,64,256]{2,0,1:T(8,128)S(1)}, f32[8,64,256]{2,0,1:T(8,128)S(1)}, f32[8,64,256]{2,0,1:T(8,128)S(1)}, f32[8,...) fusion(f32[1,64,256]{2,0,1:T(1,128)S(1)} %collective-permute-do, ...), kind=kLoop, calls=%fused_computation.63 | loop fusion | flops 5898240 | bytes 16977920 | tf_op jit(solution)/shard_map/jit(_where)/select_n | solution.py:109
  185.3 1.9 collective-permute-start.6
  187.2 8.8 %collective-permute-start.7 = (f32[1,64,256]{2,0,1:T(1,128)S(1)}, f32[1,64,256]{2,0,1:T(1,128)S(1)}, u32[]{:S(2)}, u32[]{:S(2)}) collective-permute-start(f32[1,64,256]{2,0,1:T(1,128)S(1)} %get-tuple-element.72), channel_id=1, source_target_pairs={{1,0},{2,1},{3,2},{4,3},{5,4},{6,5},{7,6},{8,7},{9,8},{10,9},{11,1... | collective-permute-start | bytes 196616 | tf_op jit(solution)/shard_map/ppermute | solution.py:26
  198.9 1.9 collective-permute-start.8
  200.8 8.8 %collective-permute-start.9 = (f32[1,64,256]{2,0,1:T(1,128)S(1)}, f32[1,64,256]{2,0,1:T(1,128)S(1)}, u32[]{:S(2)}, u32[]{:S(2)}) collective-permute-start(f32[1,64,256]{2,0,1:T(1,128)S(1)} %get-tuple-element.66), channel_id=1, source_target_pairs={{1,0},{2,1},{3,2},{4,3},{5,4},{6,5},{7,6},{8,7},{9,8},{10,9},{11,1... | collective-permute-start | bytes 196616 | tf_op jit(solution)/shard_map/ppermute | solution.py:26
  212.5 1.9 collective-permute-start.10
  214.4 8.8 %collective-permute-start.11 = (f32[1,64,256]{2,0,1:T(1,128)S(1)}, f32[1,64,256]{2,0,1:T(1,128)S(1)}, u32[]{:S(2)}, u32[]{:S(2)}) collective-permute-start(f32[1,64,256]{2,0,1:T(1,128)S(1)} %get-tuple-element.60), channel_id=1, source_target_pairs={{1,0},{2,1},{3,2},{4,3},{5,4},{6,5},{7,6},{8,7},{9,8},{10,9},{11,1... | collective-permute-start | bytes 196616 | tf_op jit(solution)/shard_map/ppermute | solution.py:26
  226.8 8.8 %collective-permute-start.12 = (f32[1,64,256]{2,0,1:T(1,128)S(1)}, f32[1,64,256]{2,0,1:T(1,128)S(1)}, u32[]{:S(2)}, u32[]{:S(2)}) collective-permute-start(f32[1,64,256]{2,0,1:T(1,128)S(1)} %copy.140), channel_id=1, source_target_pairs={{1,0},{2,1},{3,2},{4,3},{5,4},{6,5},{7,6},{8,7},{9,8},{10,9},{11,1... | collective-permute-start | bytes 196616 | tf_op jit(solution)/shard_map/ppermute | solution.py:26
  238.2 8.2 %collective-permute-done.13 = f32[1,64,256]{2,0,1:T(1,128)S(1)} collective-permute-done((f32[1,64,256]{2,0,1:T(1,128)S(1)}, f32[1,64,256]{2,0,1:T(1,128)S(1)}, u32[]{:S(2)}, u32[]{:S(2)}) %collective-permute-start.13) | collective-permute-done | bytes 65568 | tf_op jit(solution)/shard_map/ppermute | solution.py:24
  (185 shorter events, 59.3 us)
Async XLA Ops:
  3.1 35.9 %copy-start.5 = (f32[3,8,64,256]{3,1,2,0:T(8,128)}, f32[3,8,64,256]{3,1,2,0:T(8,128)S(1)}, u32[]{:S(2)}) copy-start(f32[3,8,64,256]{3,1,2,0:T(8,128)S(1)} %get-tuple-element.37) | copy-start | bytes 4718596
  8.5 142.6 %collective-permute-start = (f32[7,1,64,256]{3,1,2,0:T(1,128)}, f32[7,1,64,256]{3,1,2,0:T(1,128)}, u32[]{:S(2)}, u32[]{:S(2)}) collective-permute-start(f32[7,1,64,256]{3,1,2,0:T(1,128)} %get-tuple-element.32), channel_id=1, source_target_pairs={{0,1},{1,2},{2,3},{3,4},{4,5},{5,6},{6,7},{7,8},{8,9},{9,10},{10,1... | collective-permute-start | bytes 1376264 | tf_op jit(solution)/shard_map/ppermute | solution.py:24
  10.5 140.7 %collective-permute-start.1 = (f32[7,1,64,256]{3,1,2,0:T(1,128)}, f32[7,1,64,256]{3,1,2,0:T(1,128)}, u32[]{:S(2)}, u32[]{:S(2)}) collective-permute-start(f32[7,1,64,256]{3,1,2,0:T(1,128)} %get-tuple-element.33), channel_id=1, source_target_pairs={{1,0},{2,1},{3,2},{4,3},{5,4},{6,5},{7,6},{8,7},{9,8},{10,9},{11,1... | collective-permute-start | bytes 1376264 | tf_op jit(solution)/shard_map/ppermute | solution.py:26
  21.5 129.6 %all-to-all-start = ((f32[8,1,2,8,256]{4,3,2,1,0:T(8,128)}), f32[8,1,2,8,256]{4,3,2,1,0:T(8,128)S(1)}, u32[]{:S(2)}, u32[]{:S(2)}) async-start(f32[8,1,2,8,256]{4,3,2,1,0:T(8,128)} %stack.55), calls=%async_computation | async-start | bytes 262144 | tf_op jit(solution)/shard_map/all_to_all | solution.py:152
  28.2 147.6 %collective-permute-start.2 = (f32[1,64,256]{2,0,1:T(1,128)S(1)}, f32[1,64,256]{2,0,1:T(1,128)S(1)}, u32[]{:S(2)}, u32[]{:S(2)}) collective-permute-start(f32[1,64,256]{2,0,1:T(1,128)S(1)} %copy.122), channel_id=1, source_target_pairs={{0,1},{1,2},{2,3},{3,4},{4,5},{5,6},{6,7},{7,8},{8,9},{9,10},{10,1... | collective-permute-start | bytes 196616 | tf_op jit(solution)/shard_map/ppermute | solution.py:24
  30.2 145.6 %collective-permute-start.3 = (f32[1,64,256]{2,0,1:T(1,128)S(1)}, f32[1,64,256]{2,0,1:T(1,128)S(1)}, u32[]{:S(2)}, u32[]{:S(2)}) collective-permute-start(f32[1,64,256]{2,0,1:T(1,128)S(1)} %copy.125), channel_id=1, source_target_pairs={{1,0},{2,1},{3,2},{4,3},{5,4},{6,5},{7,6},{8,7},{9,8},{10,9},{11,1... | collective-permute-start | bytes 196616 | tf_op jit(solution)/shard_map/ppermute | solution.py:26
  55.1 82.2 %copy-start.37 = (s32[1,2]{1,0:T(1,128)S(1)}, s32[1,2]{1,0:T(1,128)}, u32[]{:S(2)}) copy-start(s32[1,2]{1,0:T(1,128)} %param.21) | copy-start | bytes 28
  55.1 82.8 %copy-start.39 = (f32[8]{0:T(128)S(1)}, f32[8]{0:T(128)}, u32[]{:S(2)}) copy-start(f32[8]{0:T(128)} %param.19) | copy-start | bytes 100
  168.6 7.1 %collective-permute-start.4 = (f32[1,64,256]{2,0,1:T(1,128)S(1)}, f32[1,64,256]{2,0,1:T(1,128)S(1)}, u32[]{:S(2)}, u32[]{:S(2)}) collective-permute-start(f32[1,64,256]{2,0,1:T(1,128)S(1)} %get-tuple-element.73), channel_id=1, source_target_pairs={{1,0},{2,1},{3,2},{4,3},{5,4},{6,5},{7,6},{8,7},{9,8},{10,9},{11,1... | collective-permute-start | bytes 196616 | tf_op jit(solution)/shard_map/ppermute | solution.py:26
  171.7 10.8 %collective-permute-start.5 = (f32[1,64,256]{2,0,1:T(1,128)S(1)}, f32[1,64,256]{2,0,1:T(1,128)S(1)}, u32[]{:S(2)}, u32[]{:S(2)}) collective-permute-start(f32[1,64,256]{2,0,1:T(1,128)S(1)} %get-tuple-element.74), channel_id=1, source_target_pairs={{0,1},{1,2},{2,3},{3,4},{4,5},{5,6},{6,7},{7,8},{8,9},{9,10},{10,1... | collective-permute-start | bytes 196616 | tf_op jit(solution)/shard_map/ppermute | solution.py:24
  174.5 8.0 %copy-start.8 = (f32[8,64,255]{2,0,1:T(8,128)S(1)}, f32[8,64,255]{2,0,1:T(8,128)}, u32[]{:S(2)}) copy-start(f32[8,64,255]{2,0,1:T(8,128)} %get-tuple-element.98) | copy-start | bytes 1566724
  174.5 8.0 %copy-start.16 = (f32[8,64,255]{2,0,1:T(8,128)S(1)}, f32[8,64,255]{2,0,1:T(8,128)}, u32[]{:S(2)}) copy-start(f32[8,64,255]{2,0,1:T(8,128)} %copy.299) | copy-start | bytes 1566724
  174.5 8.0 %copy-start.17 = (f32[8,64,255]{2,0,1:T(8,128)S(1)}, f32[8,64,255]{2,0,1:T(8,128)}, u32[]{:S(2)}) copy-start(f32[8,64,255]{2,0,1:T(8,128)} %copy.300) | copy-start | bytes 1566724
  174.5 8.0 %copy-start.28 = (f32[8,63,256]{2,0,1:T(8,128)S(1)}, f32[8,63,256]{2,0,1:T(8,128)}, u32[]{:S(2)}) copy-start(f32[8,63,256]{2,0,1:T(8,128)} %copy.301) | copy-start | bytes 1548292
  174.5 8.0 %copy-start.29 = (f32[8,63,256]{2,0,1:T(8,128)S(1)}, f32[8,63,256]{2,0,1:T(8,128)}, u32[]{:S(2)}) copy-start(f32[8,63,256]{2,0,1:T(8,128)} %copy.302) | copy-start | bytes 1548292
  185.3 10.8 %collective-permute-start.6 = (f32[1,64,256]{2,0,1:T(1,128)S(1)}, f32[1,64,256]{2,0,1:T(1,128)S(1)}, u32[]{:S(2)}, u32[]{:S(2)}) collective-permute-start(f32[1,64,256]{2,0,1:T(1,128)S(1)} %get-tuple-element.71), channel_id=1, source_target_pairs={{0,1},{1,2},{2,3},{3,4},{4,5},{5,6},{6,7},{7,8},{8,9},{9,10},{10,1... | collective-permute-start | bytes 196616 | tf_op jit(solution)/shard_map/ppermute | solution.py:24
  187.2 10.7 %collective-permute-start.7 = (f32[1,64,256]{2,0,1:T(1,128)S(1)}, f32[1,64,256]{2,0,1:T(1,128)S(1)}, u32[]{:S(2)}, u32[]{:S(2)}) collective-permute-start(f32[1,64,256]{2,0,1:T(1,128)S(1)} %get-tuple-element.72), channel_id=1, source_target_pairs={{1,0},{2,1},{3,2},{4,3},{5,4},{6,5},{7,6},{8,7},{9,8},{10,9},{11,1... | collective-permute-start | bytes 196616 | tf_op jit(solution)/shard_map/ppermute | solution.py:26
  198.9 10.8 %collective-permute-start.8 = (f32[1,64,256]{2,0,1:T(1,128)S(1)}, f32[1,64,256]{2,0,1:T(1,128)S(1)}, u32[]{:S(2)}, u32[]{:S(2)}) collective-permute-start(f32[1,64,256]{2,0,1:T(1,128)S(1)} %get-tuple-element.65), channel_id=1, source_target_pairs={{0,1},{1,2},{2,3},{3,4},{4,5},{5,6},{6,7},{7,8},{8,9},{9,10},{10,1... | collective-permute-start | bytes 196616 | tf_op jit(solution)/shard_map/ppermute | solution.py:24
  200.8 10.7 %collective-permute-start.9 = (f32[1,64,256]{2,0,1:T(1,128)S(1)}, f32[1,64,256]{2,0,1:T(1,128)S(1)}, u32[]{:S(2)}, u32[]{:S(2)}) collective-permute-start(f32[1,64,256]{2,0,1:T(1,128)S(1)} %get-tuple-element.66), channel_id=1, source_target_pairs={{1,0},{2,1},{3,2},{4,3},{5,4},{6,5},{7,6},{8,7},{9,8},{10,9},{11,1... | collective-permute-start | bytes 196616 | tf_op jit(solution)/shard_map/ppermute | solution.py:26
  212.5 10.8 %collective-permute-start.10 = (f32[1,64,256]{2,0,1:T(1,128)S(1)}, f32[1,64,256]{2,0,1:T(1,128)S(1)}, u32[]{:S(2)}, u32[]{:S(2)}) collective-permute-start(f32[1,64,256]{2,0,1:T(1,128)S(1)} %get-tuple-element.59), channel_id=1, source_target_pairs={{0,1},{1,2},{2,3},{3,4},{4,5},{5,6},{6,7},{7,8},{8,9},{9,10},{10,1... | collective-permute-start | bytes 196616 | tf_op jit(solution)/shard_map/ppermute | solution.py:24
  214.4 10.7 %collective-permute-start.11 = (f32[1,64,256]{2,0,1:T(1,128)S(1)}, f32[1,64,256]{2,0,1:T(1,128)S(1)}, u32[]{:S(2)}, u32[]{:S(2)}) collective-permute-start(f32[1,64,256]{2,0,1:T(1,128)S(1)} %get-tuple-element.60), channel_id=1, source_target_pairs={{1,0},{2,1},{3,2},{4,3},{5,4},{6,5},{7,6},{8,7},{9,8},{10,9},{11,1... | collective-permute-start | bytes 196616 | tf_op jit(solution)/shard_map/ppermute | solution.py:26
  226.8 11.4 %collective-permute-start.12 = (f32[1,64,256]{2,0,1:T(1,128)S(1)}, f32[1,64,256]{2,0,1:T(1,128)S(1)}, u32[]{:S(2)}, u32[]{:S(2)}) collective-permute-start(f32[1,64,256]{2,0,1:T(1,128)S(1)} %copy.140), channel_id=1, source_target_pairs={{1,0},{2,1},{3,2},{4,3},{5,4},{6,5},{7,6},{8,7},{9,8},{10,9},{11,1... | collective-permute-start | bytes 196616 | tf_op jit(solution)/shard_map/ppermute | solution.py:26
  235.7 10.7 %collective-permute-start.13 = (f32[1,64,256]{2,0,1:T(1,128)S(1)}, f32[1,64,256]{2,0,1:T(1,128)S(1)}, u32[]{:S(2)}, u32[]{:S(2)}) collective-permute-start(f32[1,64,256]{2,0,1:T(1,128)S(1)} %copy.142), channel_id=1, source_target_pairs={{0,1},{1,2},{2,3},{3,4},{4,5},{5,6},{6,7},{7,8},{8,9},{9,10},{10,1... | collective-permute-start | bytes 196616 | tf_op jit(solution)/shard_map/ppermute | solution.py:24
  238.0 8.8 %copy-start.15 = (f32[8,64,256]{2,1,0:T(8,128)S(1)}, f32[8,64,256]{2,1,0:T(8,128)}, u32[]{:S(2)}) copy-start(f32[8,64,256]{2,1,0:T(8,128)} %copy.119) | copy-start | bytes 1572868
  (31 other events, 91.3 us)
